TPU v7x, 512 devices: a whole 4x4x16 slice. The times are simulated.
512 devices in a mesh: section: 4 (over x_hi, core), ctx: 32 (over x_lo, z), dp: 4 (over y).
Axes of the slice: x: 4 (x_hi: 2, x_lo: 2; x = x_hi * 2 + x_lo), y: 4, z: 16, core: 2. Of those that a mesh axis runs over, the one named last changes fastest.
Arguments:
- inputs: bfloat16 [4, 8192, 4096], P('section', 'ctx', 'dp'), may hold values from -6 to 6
- upstream: bfloat16 [4, 8192, 4096], P('section', 'ctx', 'dp'), may hold values from -6 to 6
- short_filter: bfloat16 [4, 21, 256], P('section', None, 'dp'), may hold values from -2 to 2
- medium_filter: bfloat16 [4, 128, 256], P('section', None, 'dp'), may hold values from -0.5 to 0.5
Outputs:
- incoming: bfloat16 [4, 8192, 4096], P('section', 'ctx', 'dp')
- grad_short: float32 [4, 21, 256], P('section', None, ('dp', 'ctx'))
- grad_medium: float32 [4, 128, 256], P('section', None, ('dp', 'ctx'))
All inputs are finite; a program needn't handle non-finite values.
Results may differ from a plain program's by a relative error of at most 0.0071.
Values may be sent and summed in bfloat16 or wider, within the bound.
No kernel may reach another device: no remote copies, remote signals or barrier semaphores. Data moves between devices by JAX's collectives and lax.ppermute only.
A program may use at most 64 MiB of HBM per device.

v0:
```python
from functools import partial

import jax
import jax.numpy as jnp
from jax import lax
from jax.sharding import PartitionSpec as P


def passed_along(block, axis, distance):
    devices = range(lax.axis_size(axis))
    route = [(i - distance, i) for i in devices if i - distance in devices]
    return lax.ppermute(block, axis, route)


def band_matrix(filter_taps, out_rows):
    tap_count, group_count = filter_taps.shape
    leading = jnp.flip(filter_taps, 0).T
    padded = jnp.concatenate([leading, jnp.zeros((group_count, out_rows), filter_taps.dtype)], 1)
    span_len = out_rows + tap_count - 1
    tiled_rows = jnp.tile(padded, (1, out_rows))[:, : out_rows * span_len]
    return tiled_rows.reshape(group_count, out_rows, span_len)


def diagonal_sums(cross_terms, tap_count):
    group_count, out_rows, span_len = cross_terms.shape
    flat_view = jnp.pad(
        cross_terms.reshape(group_count, out_rows * span_len), ((0, 0), (0, out_rows))
    )
    skewed = flat_view.reshape(group_count, out_rows, span_len + 1)
    return jnp.flip(jnp.sum(skewed[:, :, :tap_count], axis=1), 1)


def short_features(padded, chan_short, out_rows):
    lag_count = chan_short.shape[1]
    running = jnp.zeros((3, out_rows, padded.shape[1]), jnp.float32)
    for offset in range(lag_count):
        first_row = lag_count - 1 - offset
        running = running + chan_short[:, offset, None, :] * padded[
            None, first_row : first_row + out_rows
        ].astype(jnp.float32)
    return running.astype(jnp.bfloat16)


def medium_block(operands, row_block):
    filter_blk, kv_blk, gate_blk = operands
    tap_count = filter_blk.shape[0]
    seq_rows = gate_blk.shape[0] - tap_count + 1
    span_len = row_block + tap_count - 1
    toeplitz = band_matrix(filter_blk, row_block)

    def row_part(start):
        kv_win = lax.dynamic_slice_in_dim(kv_blk, start, span_len, 0)
        gate_win = lax.dynamic_slice_in_dim(gate_blk, start, span_len, 0)
        gate_rows = gate_win[:row_block]
        mixed_out = jnp.einsum("gts,sgc->tgc", toeplitz, kv_win, preferred_element_type=jnp.float32)
        back_out = jnp.flip(
            jnp.einsum(
                "gts,sgc->tgc", toeplitz, jnp.flip(gate_win, 0), preferred_element_type=jnp.float32
            ),
            0,
        )
        cross_terms = jnp.einsum(
            "tgc,sgc->gts", gate_rows, kv_win, preferred_element_type=jnp.float32
        )
        return (mixed_out, back_out, diagonal_sums(cross_terms, tap_count).T)

    starts = jnp.arange(seq_rows // row_block, dtype=jnp.int32) * row_block
    mixed_out, back_out, taps_grad = lax.map(row_part, starts)
    full_shape = (seq_rows,) + mixed_out.shape[2:]
    return (mixed_out.reshape(full_shape), back_out.reshape(full_shape), jnp.sum(taps_grad, 0))


def split_groups(values_in, block_count, group_width):
    length = values_in.shape[0]
    return values_in.reshape(length, block_count, -1, group_width).transpose(1, 0, 2, 3)


def join_groups(blocks):
    block_count, length, block_groups, group_width = blocks.shape
    return blocks.transpose(1, 0, 2, 3).reshape(length, block_count * block_groups * group_width)


def per_device(inputs, upstream, short_filter, medium_filter):
    signal = inputs[0]
    grad_out = upstream[0]
    seq_rows, chan_count = signal.shape
    tap_count = medium_filter.shape[1]
    group_count = medium_filter.shape[2]
    lag_count = short_filter.shape[1] // 3
    group_width = chan_count // group_count
    short_rim = lag_count - 1
    medium_rim = tap_count - 1
    chan_short = jnp.broadcast_to(
        short_filter[0].astype(jnp.float32).reshape(3, lag_count, group_count, 1),
        (3, lag_count, group_count, group_width),
    ).reshape(3, lag_count, chan_count)
    medium_taps = medium_filter[0]
    zero_rim = jnp.zeros((short_rim, chan_count), jnp.bfloat16)
    features_local = short_features(jnp.concatenate([zero_rim, signal], 0), chan_short, seq_rows)
    kv_local = (
        features_local[1].astype(jnp.float32) * features_local[2].astype(jnp.float32)
    ).astype(jnp.bfloat16)
    signal_rim, kv_rim = passed_along(
        (signal[seq_rows - short_rim :], kv_local[seq_rows - medium_rim :]), "ctx", 1
    )
    signal_pad = jnp.concatenate([signal_rim, signal], 0)
    head_features = short_features(signal_pad[: 2 * short_rim], chan_short, short_rim)
    features = jnp.concatenate([head_features, features_local[:, short_rim:]], 1)
    query_in = features[0]
    key_in = features[1]
    value_in = features[2]
    head_products = (
        key_in[:short_rim].astype(jnp.float32) * value_in[:short_rim].astype(jnp.float32)
    ).astype(jnp.bfloat16)
    products = jnp.concatenate([head_products, kv_local[short_rim:]], 0)
    kv_pad = jnp.concatenate([kv_rim, products], 0)
    gate_grad = (grad_out.astype(jnp.float32) * query_in.astype(jnp.float32)).astype(jnp.bfloat16)
    gate_rim = passed_along(gate_grad[:medium_rim], "ctx", -1)
    gate_ext = jnp.concatenate([gate_grad, gate_rim], 0)
    block_groups = 8
    block_count = group_count // block_groups
    row_block = 128
    taps_blocks = medium_taps.reshape(tap_count, block_count, block_groups).transpose(1, 0, 2)
    mixed_blocks, back_blocks, grad_blocks = lax.map(
        partial(medium_block, row_block=row_block),
        (
            taps_blocks,
            split_groups(kv_pad, block_count, group_width),
            split_groups(gate_ext, block_count, group_width),
        ),
    )
    mixed_out = join_groups(mixed_blocks)
    back_out = join_groups(back_blocks)
    taps_grad = grad_blocks.transpose(1, 0, 2).reshape(tap_count, group_count)
    query_grad = (grad_out.astype(jnp.float32) * mixed_out).astype(jnp.bfloat16)
    key_grad = (back_out * value_in.astype(jnp.float32)).astype(jnp.bfloat16)
    value_grad = (back_out * key_in.astype(jnp.float32)).astype(jnp.bfloat16)
    feature_grads = jnp.stack([query_grad, key_grad, value_grad])
    feature_rim = passed_along(feature_grads[:, :short_rim], "ctx", -1)
    grads_pad = jnp.concatenate([feature_grads, feature_rim], 1)
    running = jnp.zeros((seq_rows, chan_count), jnp.float32)
    short_rows = []
    for offset in range(lag_count):
        running = running + jnp.sum(
            chan_short[:, offset, None, :]
            * grads_pad[:, offset : offset + seq_rows].astype(jnp.float32),
            axis=0,
        )
        lag_start = short_rim - offset
        short_rows.append(
            jnp.sum(
                feature_grads.astype(jnp.float32)
                * signal_pad[None, lag_start : lag_start + seq_rows].astype(jnp.float32),
                axis=1,
            )
        )
    input_grad = running.astype(jnp.bfloat16)
    short_grad = jnp.stack(short_rows, 1).reshape(3 * lag_count, group_count, group_width).sum(-1)
    short_part, medium_part = (
        lax.psum_scatter(short_grad[None], "ctx", scatter_dimension=2, tiled=True),
        lax.psum_scatter(taps_grad[None], "ctx", scatter_dimension=2, tiled=True),
    )
    incoming = passed_along(input_grad[None], "section", -1)
    return (incoming, short_part, medium_part)


def solution(mesh):
    in_specs = (
        P("section", "ctx", "dp"),
        P("section", "ctx", "dp"),
        P("section", None, "dp"),
        P("section", None, "dp"),
    )
    out_specs = (
        P("section", "ctx", "dp"),
        P("section", None, ("dp", "ctx")),
        P("section", None, ("dp", "ctx")),
    )
    return jax.shard_map(
        per_device, mesh=mesh, in_specs=in_specs, out_specs=out_specs, check_vma=False
    )
```

profile of v0, /device:TPU:14, one launch (start us, length us, event | category | flops | bytes accessed | tf_op | source)
XLA Modules:
  0.0 344.5 jit_solution(14716858355347633938)
XLA Ops:
  1.4 4.0 %collective-permute-start.1 = (bf16[6,1024]{1,0:T(8,128)(2,1)S(1)}, bf16[6,1024]{1,0:T(8,128)(2,1)S(1)}, u32[]{:S(2)}, u32[]{:S(2)}) collective-permute-start(bf16[6,1024]{1,0:T(8,128)(2,1)S(1)} %get-tuple-element.288), channel_id=1, source_target_pairs={{0,4},{4,8},{8,12},{12,16},{16,20},{20,24},{24,28},{28,32},{32,36}... | collective-permute-start | bytes 36872 | tf_op jit(solution)/shard_map/ppermute | solution.py:12
  7.3 7.6 %collective-permute-done.1 = bf16[6,1024]{1,0:T(8,128)(2,1)S(1)} collective-permute-done((bf16[6,1024]{1,0:T(8,128)(2,1)S(1)}, bf16[6,1024]{1,0:T(8,128)(2,1)S(1)}, u32[]{:S(2)}, u32[]{:S(2)}) %collective-permute-start.1) | collective-permute-done | bytes 12320 | tf_op jit(solution)/shard_map/ppermute | solution.py:12
  14.9 3.0 fusion.21
  17.9 1.5 add_convert_fusion
  21.5 3.9 %collective-permute-start.2 = (bf16[127,1024]{1,0:T(8,128)(2,1)S(1)}, bf16[127,1024]{1,0:T(8,128)(2,1)S(1)}, u32[]{:S(2)}, u32[]{:S(2)}) collective-permute-start(bf16[127,1024]{1,0:T(8,128)(2,1)S(1)} %slice_bitcast_fusion.1), channel_id=1, source_target_pairs={{4,0},{8,4},{12,8},{16,12},{20,16},{24,20},{28,24},{32,28},{36,32}... | collective-permute-start | bytes 780296 | tf_op jit(solution)/shard_map/ppermute | solution.py:12
  25.6 1.9 collective-permute-start
  27.6 3.0 collective-permute-done.2
  31.8 4.5 %collective-permute-done = bf16[127,1024]{1,0:T(8,128)(2,1)S(1)} collective-permute-done((bf16[127,1024]{1,0:T(8,128)(2,1)S(1)}, bf16[127,1024]{1,0:T(8,128)(2,1)S(1)}, u32[]{:S(2)}, u32[]{:S(2)}) %collective-permute-start) | collective-permute-done | bytes 260128 | tf_op jit(solution)/shard_map/ppermute | solution.py:12
  37.6 160.2 %while.46 = (s32[]{:T(128)}, f32[8,256,8,16]{1,3,2,0:T(8,128)}, f32[8,256,8,16]{1,3,2,0:T(8,128)}, f32[8,128,8]{1,2,0:T(8,128)S(1)}, bf16[8,383,8,16]{1,3,2,0:T(...) while((s32[]{:T(128)}, f32[8,256,8,16]{1,3,2,0:T(8,128)}, ...), condition=%wide.region_5.6_spmd, body=%wide.region_0.5_spmd.sunk | while | flops 25198600 | bytes 11928522 | solution.py:124
  39.4 1.4 reshape.192
  40.8 15.2 %while.47 = (s32[]{:T(128)}, f32[2,128,8,16]{1,0,3,2:T(2,128)S(1)}, f32[2,128,8,16]{1,0,3,2:T(2,128)S(1)}, f32[2,128,8]{1,2,0:T(8,128)S(1)}, s32[2]{0:T(128)S(1)...) while((s32[]{:T(128)}, f32[2,128,8,16]{1,0,3,2:T(2,128)S(1)}, ...), condition=%wide.region_3.3_spmd, body=%wide.region_1.2_spmd.sunk | while | flops 25197572 | bytes 7834299 | solution.py:68
  45.4 1.3 dynamic_update_slice.55
  47.1 1.4 dynamic_update_slice.54
  53.0 1.3 dynamic_update_slice.55
  54.7 1.4 dynamic_update_slice.54
  59.4 1.4 reshape.192
  60.8 15.2 %while.47 = (s32[]{:T(128)}, f32[2,128,8,16]{1,0,3,2:T(2,128)S(1)}, f32[2,128,8,16]{1,0,3,2:T(2,128)S(1)}, f32[2,128,8]{1,2,0:T(8,128)S(1)}, s32[2]{0:T(128)S(1)...) while((s32[]{:T(128)}, f32[2,128,8,16]{1,0,3,2:T(2,128)S(1)}, ...), condition=%wide.region_3.3_spmd, body=%wide.region_1.2_spmd.sunk | while | flops 25197572 | bytes 7834299 | solution.py:68
  65.5 1.3 dynamic_update_slice.55
  67.1 1.4 dynamic_update_slice.54
  73.1 1.3 dynamic_update_slice.55
  74.7 1.4 dynamic_update_slice.54
  79.4 1.4 reshape.192
  80.9 15.2 %while.47 = (s32[]{:T(128)}, f32[2,128,8,16]{1,0,3,2:T(2,128)S(1)}, f32[2,128,8,16]{1,0,3,2:T(2,128)S(1)}, f32[2,128,8]{1,2,0:T(8,128)S(1)}, s32[2]{0:T(128)S(1)...) while((s32[]{:T(128)}, f32[2,128,8,16]{1,0,3,2:T(2,128)S(1)}, ...), condition=%wide.region_3.3_spmd, body=%wide.region_1.2_spmd.sunk | while | flops 25197572 | bytes 7834299 | solution.py:68
  85.5 1.3 dynamic_update_slice.55
  87.1 1.4 dynamic_update_slice.54
  93.1 1.3 dynamic_update_slice.55
  94.7 1.4 dynamic_update_slice.54
  99.5 1.4 reshape.192
  100.9 15.2 %while.47 = (s32[]{:T(128)}, f32[2,128,8,16]{1,0,3,2:T(2,128)S(1)}, f32[2,128,8,16]{1,0,3,2:T(2,128)S(1)}, f32[2,128,8]{1,2,0:T(8,128)S(1)}, s32[2]{0:T(128)S(1)...) while((s32[]{:T(128)}, f32[2,128,8,16]{1,0,3,2:T(2,128)S(1)}, ...), condition=%wide.region_3.3_spmd, body=%wide.region_1.2_spmd.sunk | while | flops 25197572 | bytes 7834299 | solution.py:68
  105.5 1.3 dynamic_update_slice.55
  107.1 1.4 dynamic_update_slice.54
  114.7 1.4 dynamic_update_slice.54
  119.5 1.4 reshape.192
  120.9 15.2 %while.47 = (s32[]{:T(128)}, f32[2,128,8,16]{1,0,3,2:T(2,128)S(1)}, f32[2,128,8,16]{1,0,3,2:T(2,128)S(1)}, f32[2,128,8]{1,2,0:T(8,128)S(1)}, s32[2]{0:T(128)S(1)...) while((s32[]{:T(128)}, f32[2,128,8,16]{1,0,3,2:T(2,128)S(1)}, ...), condition=%wide.region_3.3_spmd, body=%wide.region_1.2_spmd.sunk | while | flops 25197572 | bytes 7834299 | solution.py:68
  127.2 1.4 dynamic_update_slice.54
  133.1 1.3 dynamic_update_slice.55
  134.8 1.4 dynamic_update_slice.54
  139.5 1.4 reshape.192
  140.9 15.2 %while.47 = (s32[]{:T(128)}, f32[2,128,8,16]{1,0,3,2:T(2,128)S(1)}, f32[2,128,8,16]{1,0,3,2:T(2,128)S(1)}, f32[2,128,8]{1,2,0:T(8,128)S(1)}, s32[2]{0:T(128)S(1)...) while((s32[]{:T(128)}, f32[2,128,8,16]{1,0,3,2:T(2,128)S(1)}, ...), condition=%wide.region_3.3_spmd, body=%wide.region_1.2_spmd.sunk | while | flops 25197572 | bytes 7834299 | solution.py:68
  145.5 1.3 dynamic_update_slice.55
  147.2 1.4 dynamic_update_slice.54
  153.2 1.3 dynamic_update_slice.55
  154.8 1.4 dynamic_update_slice.54
  159.5 1.4 reshape.192
  160.9 15.2 %while.47 = (s32[]{:T(128)}, f32[2,128,8,16]{1,0,3,2:T(2,128)S(1)}, f32[2,128,8,16]{1,0,3,2:T(2,128)S(1)}, f32[2,128,8]{1,2,0:T(8,128)S(1)}, s32[2]{0:T(128)S(1)...) while((s32[]{:T(128)}, f32[2,128,8,16]{1,0,3,2:T(2,128)S(1)}, ...), condition=%wide.region_3.3_spmd, body=%wide.region_1.2_spmd.sunk | while | flops 25197572 | bytes 7834299 | solution.py:68
  165.6 1.3 dynamic_update_slice.55
  167.2 1.4 dynamic_update_slice.54
  173.2 1.3 dynamic_update_slice.55
  174.8 1.4 dynamic_update_slice.54
  179.5 1.4 reshape.192
  181.0 15.2 %while.47 = (s32[]{:T(128)}, f32[2,128,8,16]{1,0,3,2:T(2,128)S(1)}, f32[2,128,8,16]{1,0,3,2:T(2,128)S(1)}, f32[2,128,8]{1,2,0:T(8,128)S(1)}, s32[2]{0:T(128)S(1)...) while((s32[]{:T(128)}, f32[2,128,8,16]{1,0,3,2:T(2,128)S(1)}, ...), condition=%wide.region_3.3_spmd, body=%wide.region_1.2_spmd.sunk | while | flops 25197572 | bytes 7834299 | solution.py:68
  187.2 1.4 dynamic_update_slice.54
  193.2 1.3 dynamic_update_slice.55
  194.8 1.4 dynamic_update_slice.54
  197.7 2.7 copy.27
  200.4 1.6 multiply_convert_fusion.1
  202.0 2.7 copy.26
  204.7 1.6 fusion.16
  206.6 2.2 collective-permute-start.3
  208.9 2.1 fusion.11
  211.0 1.7 collective-permute-done.3
  212.9 3.6 %multiply_reduce_fusion.5 = (f32[256,1024]{1,0:T(8,128)S(1)}, f32[256,1024]{1,0:T(8,128)S(1)}, f32[256,1024]{1,0:T(8,128)S(1)}, f32[256,1024]{1,0:T(8,128)S(1)},...) fusion(bf16[3,262,1024]{2,1,0:T(8,128)(2,1)S(1)} %pad_maximum_fusion, f32[3,1024]{1,0:T(4,128)S(1)} %get-tuple-element.302, ...), kind=kLoop, calls=%fused_computation.39 | loop fusion | flops 12582912 | bytes 15802368 | tf_op jit(solution)/shard_map/reduce_sum | solution.py:144
  217.3 1.9 collective-permute-start.4
  222.0 120.5 %all-reduce.5 = (f32[1,21,64]{1,2,0:T(8,128)S(1)}, f32[1,128,64]{1,2,0:T(8,128)S(1)}) all-reduce(f32[1,21,64]{1,2,0:T(8,128)S(1)} %copy.29, f32[1,128,64]{1,2,0:T(8,128)S(1)} %bitcast.135), channel_id=2, replica_groups=mesh['section'=4,'ctx'=32,'dp'=4] {'ctx'}, use_global_device_ids=true, to_apply=%region_21.22.clone | all-reduce | flops 9536 | bytes 76288
  (395 shorter events, 90.1 us)
Async XLA Ops:
  0.6 5.9 %copy-start.12 = (bf16[1,21,64]{2,1,0:T(8,128)(2,1)S(1)}, bf16[1,21,64]{2,1,0:T(8,128)(2,1)}, u32[]{:S(2)}) copy-start(bf16[1,21,64]{2,1,0:T(8,128)(2,1)} %param.10) | copy-start | bytes 8068
  1.4 13.5 %copy-start.4 = (bf16[1,256,1024]{2,1,0:T(8,128)(2,1)S(1)}, bf16[1,256,1024]{2,1,0:T(8,128)(2,1)}, u32[]{:S(2)}) copy-start(bf16[1,256,1024]{2,1,0:T(8,128)(2,1)} %param.8) | copy-start | bytes 1572868
  1.4 13.5 %collective-permute-start.1 = (bf16[6,1024]{1,0:T(8,128)(2,1)S(1)}, bf16[6,1024]{1,0:T(8,128)(2,1)S(1)}, u32[]{:S(2)}, u32[]{:S(2)}) collective-permute-start(bf16[6,1024]{1,0:T(8,128)(2,1)S(1)} %get-tuple-element.288), channel_id=1, source_target_pairs={{0,4},{4,8},{8,12},{12,16},{16,20},{20,24},{24,28},{28,32},{32,36}... | collective-permute-start | bytes 36872 | tf_op jit(solution)/shard_map/ppermute | solution.py:12
  6.5 11.4 %copy-start.2 = (f32[256,1024]{1,0:T(8,128)}, f32[256,1024]{1,0:T(8,128)S(1)}, u32[]{:S(2)}) copy-start(f32[256,1024]{1,0:T(8,128)S(1)} %bitcast_convert_fusion.1) | copy-start | bytes 3145732
  19.8 1.7 copy-start
  19.8 1.4 copy-start.11
  21.5 9.1 %collective-permute-start.2 = (bf16[127,1024]{1,0:T(8,128)(2,1)S(1)}, bf16[127,1024]{1,0:T(8,128)(2,1)S(1)}, u32[]{:S(2)}, u32[]{:S(2)}) collective-permute-start(bf16[127,1024]{1,0:T(8,128)(2,1)S(1)} %slice_bitcast_fusion.1), channel_id=1, source_target_pairs={{4,0},{8,4},{12,8},{16,12},{20,16},{24,20},{28,24},{32,28},{36,32}... | collective-permute-start | bytes 780296 | tf_op jit(solution)/shard_map/ppermute | solution.py:12
  25.6 10.6 %collective-permute-start = (bf16[127,1024]{1,0:T(8,128)(2,1)S(1)}, bf16[127,1024]{1,0:T(8,128)(2,1)S(1)}, u32[]{:S(2)}, u32[]{:S(2)}) collective-permute-start(bf16[127,1024]{1,0:T(8,128)(2,1)S(1)} %slice_bitcast_fusion.2), channel_id=1, source_target_pairs={{0,4},{4,8},{8,12},{12,16},{16,20},{20,24},{24,28},{28,32},{32,36}... | collective-permute-start | bytes 780296 | tf_op jit(solution)/shard_map/ppermute | solution.py:12
  197.7 2.7 copy-start.1
  202.0 6.8 %copy-start.9 = (f32[256,1024]{1,0:T(8,128)S(1)}, f32[256,1024]{1,0:T(8,128)}, u32[]{:S(2)}) copy-start(f32[256,1024]{1,0:T(8,128)} %get-tuple-element.274) | copy-start | bytes 3145732
  202.0 6.8 %copy-start.10 = (f32[256,1024]{1,0:T(8,128)S(1)}, f32[256,1024]{1,0:T(8,128)}, u32[]{:S(2)}) copy-start(f32[256,1024]{1,0:T(8,128)} %get-tuple-element.275) | copy-start | bytes 3145732
  204.7 4.1 %copy-start.7 = (f32[256,1024]{1,0:T(8,128)S(1)}, f32[256,1024]{1,0:T(8,128)}, u32[]{:S(2)}) copy-start(f32[256,1024]{1,0:T(8,128)} %get-tuple-element.272) | copy-start | bytes 3145732
  204.7 4.2 %copy-start.8 = (f32[256,1024]{1,0:T(8,128)S(1)}, f32[256,1024]{1,0:T(8,128)}, u32[]{:S(2)}) copy-start(f32[256,1024]{1,0:T(8,128)} %get-tuple-element.273) | copy-start | bytes 3145732
  206.4 2.5 copy-start.3
  206.4 2.5 copy-start.5
  206.4 2.5 copy-start.6
  206.6 6.1 %collective-permute-start.3 = (bf16[3,6,1024]{2,1,0:T(8,128)(2,1)S(1)}, bf16[3,6,1024]{2,1,0:T(8,128)(2,1)S(1)}, u32[]{:S(2)}, u32[]{:S(2)}) collective-permute-start(bf16[3,6,1024]{2,1,0:T(8,128)(2,1)S(1)} %slice.262), channel_id=1, source_target_pairs={{4,0},{8,4},{12,8},{16,12},{20,16},{24,20},{28,24},{32,28},{36,32}... | collective-permute-start | bytes 110600 | tf_op jit(solution)/shard_map/ppermute | solution.py:12
  217.3 126.4 %collective-permute-start.4 = (bf16[1,256,1024]{2,1,0:T(8,128)(2,1)S(1)}, bf16[1,256,1024]{2,1,0:T(8,128)(2,1)S(1)}, u32[]{:S(2)}, u32[]{:S(2)}) collective-permute-start(bf16[1,256,1024]{2,1,0:T(8,128)(2,1)S(1)} %fusion.17), channel_id=1, source_target_pairs={{128,0},{256,128},{384,256},{129,1},{257,129},{385,257},{130,2},{2... | collective-permute-start | bytes 1572872 | tf_op jit(solution)/shard_map/ppermute | solution.py:12
where the time goes:
time: 346 us; the launch traced here: 344 us
  local copies, waits for them, and re-layouts  123 us (36%)
  blocking collectives  121 us (35%)
  loops' own time  32.7 us (9%)
  other arithmetic  19.7 us (6%)
  waiting for transfers between devices  16.7 us (5%)
  matrix products  16 us (5%)
  starting transfers between devices  14 us (4%)
    unnamed x1, blocking collectives  121 us
    dynamic_update_slice x48, local copies, waits for them, and re-layouts, medium_block(): mixed_out, back_out, taps_grad = lax.map(row_part, starts)  43.1 us
    another operation x8, loops' own time, medium_block(): mixed_out, back_out, taps_grad = lax.map(row_part, starts)  32.1 us
    ppermute x5, waiting for transfers between devices, passed_along(): return lax.ppermute(block, axis, route)  16.7 us
    ppermute x5, starting transfers between devices, passed_along(): return lax.ppermute(block, axis, route)  14 us
    squeeze x16, local copies, waits for them, and re-layouts, per_device(): lax.map(partial(medium_block, row_block=row_block), (taps_blocks, split_g...  13.2 us
    reshape x8, local copies, waits for them, and re-layouts, band_matrix(): return tiled_rows.reshape(group_count, out_rows, span_len)  10.9 us
    dynamic_update_slice x24, local copies, waits for them, and re-layouts, per_device(): lax.map(partial(medium_block, row_block=row_block), (taps_blocks, split_g...  10.7 us
  transfers between devices with their start and end apart: 5, of which 4 were waited for; matrix products, arithmetic and copies ran while one was open for 2% of the time, Pallas kernels for 0%

commit v1 on v0

--- a/solution.py
+++ b/solution.py
@@ -10,6 +10,15 @@
     devices = range(lax.axis_size(axis))
     route = [(i - distance, i) for i in devices if i - distance in devices]
     return lax.ppermute(block, axis, route)
+
+
+def owned_sum(partial_terms, axis):
+    axis_len = lax.axis_size(axis)
+    row_count, col_count = partial_terms.shape
+    blocks = partial_terms.reshape(row_count, axis_len, col_count // axis_len)
+    gathered = lax.all_gather(blocks, axis, axis=0, tiled=False)
+    mine = lax.dynamic_index_in_dim(gathered, lax.axis_index(axis), axis=2, keepdims=False)
+    return jnp.sum(mine, axis=0)
 
 
 def band_matrix(filter_taps, out_rows):
@@ -156,10 +165,8 @@
         )
     input_grad = running.astype(jnp.bfloat16)
     short_grad = jnp.stack(short_rows, 1).reshape(3 * lag_count, group_count, group_width).sum(-1)
-    short_part, medium_part = (
-        lax.psum_scatter(short_grad[None], "ctx", scatter_dimension=2, tiled=True),
-        lax.psum_scatter(taps_grad[None], "ctx", scatter_dimension=2, tiled=True),
-    )
+    short_part = owned_sum(short_grad, "ctx")[None]
+    medium_part = owned_sum(taps_grad, "ctx")[None]
     incoming = passed_along(input_grad[None], "section", -1)
     return (incoming, short_part, medium_part)
 

time: 346 us -> 353 us (1.020)
  the two profiles are of different devices: /device:TPU:14 before, /device:TPU:8 now
where the time goes in v1:
time: 353 us; the launch traced here: 351 us
  local copies, waits for them, and re-layouts  121 us (34%)
  blocking collectives  75.1 us (21%)
  waiting for transfers between devices  56.9 us (16%)
  loops' own time  32.7 us (9%)
  other arithmetic  22.5 us (6%)
  matrix products  16 us (5%)
  between operations  14.5 us (4%)
  starting transfers between devices  12.7 us (4%)
    all_gather x1, blocking collectives, owned_sum(): gathered = lax.all_gather(blocks, axis, axis=0, tiled=False)  75.1 us
    all_gather x1, waiting for transfers between devices, owned_sum(): gathered = lax.all_gather(blocks, axis, axis=0, tiled=False)  52.6 us
    dynamic_update_slice x48, local copies, waits for them, and re-layouts, medium_block(): mixed_out, back_out, taps_grad = lax.map(row_part, starts)  43.1 us
    another operation x8, loops' own time, medium_block(): mixed_out, back_out, taps_grad = lax.map(row_part, starts)  32.1 us
    squeeze x16, local copies, waits for them, and re-layouts, per_device(): lax.map(partial(medium_block, row_block=row_block), (taps_blocks, split_g...  13.2 us
    ppermute x5, starting transfers between devices, passed_along(): return lax.ppermute(block, axis, route)  12.7 us
    reshape x8, local copies, waits for them, and re-layouts, band_matrix(): return tiled_rows.reshape(group_count, out_rows, span_len)  10.9 us
    dynamic_update_slice x24, local copies, waits for them, and re-layouts, per_device(): lax.map(partial(medium_block, row_block=row_block), (taps_blocks, split_g...  10.7 us
  transfers between devices with their start and end apart: 6, of which 4 were waited for; matrix products, arithmetic and copies ran while one was open for 4% of the time, Pallas kernels for 0%

profile of v1, /device:TPU:8, one launch (start us, length us, event | category | flops | bytes accessed | tf_op | source)
XLA Modules:
  0.0 351.3 jit_solution(14208260657527814230)
XLA Ops:
  8.0 4.0 %collective-permute-start.1 = (bf16[6,1024]{1,0:T(8,128)(2,1)S(1)}, bf16[6,1024]{1,0:T(8,128)(2,1)S(1)}, u32[]{:S(2)}, u32[]{:S(2)}) collective-permute-start(bf16[6,1024]{1,0:T(8,128)(2,1)S(1)} %get-tuple-element.286), channel_id=1, source_target_pairs={{0,4},{4,8},{8,12},{12,16},{16,20},{20,24},{24,28},{28,32},{32,36}... | collective-permute-start | bytes 36872 | tf_op jit(solution)/shard_map/ppermute | solution.py:12
  13.9 3.1 fusion.21
  17.0 1.5 add_convert_fusion
  20.5 1.3 collective-permute-start.2
  22.0 4.6 %collective-permute-start = (bf16[127,1024]{1,0:T(8,128)(2,1)S(1)}, bf16[127,1024]{1,0:T(8,128)(2,1)S(1)}, u32[]{:S(2)}, u32[]{:S(2)}) collective-permute-start(bf16[127,1024]{1,0:T(8,128)(2,1)S(1)} %slice_bitcast_fusion.2), channel_id=1, source_target_pairs={{0,4},{4,8},{8,12},{12,16},{16,20},{20,24},{24,28},{28,32},{32,36}... | collective-permute-start | bytes 780296 | tf_op jit(solution)/shard_map/ppermute | solution.py:12
  26.6 3.8 %collective-permute-done.2 = bf16[127,1024]{1,0:T(8,128)(2,1)S(1)} collective-permute-done((bf16[127,1024]{1,0:T(8,128)(2,1)S(1)}, bf16[127,1024]{1,0:T(8,128)(2,1)S(1)}, u32[]{:S(2)}, u32[]{:S(2)}) %collective-permute-start.2) | collective-permute-done | bytes 260128 | tf_op jit(solution)/shard_map/ppermute | solution.py:12
  33.1 160.2 %while.46 = (s32[]{:T(128)}, f32[8,256,8,16]{1,3,2,0:T(8,128)}, f32[8,256,8,16]{1,3,2,0:T(8,128)}, f32[8,128,8]{1,2,0:T(8,128)S(1)}, bf16[8,383,8,16]{1,3,2,0:T(...) while((s32[]{:T(128)}, f32[8,256,8,16]{1,3,2,0:T(8,128)}, ...), condition=%wide.region_5.6_spmd, body=%wide.region_0.5_spmd.sunk | while | flops 25198600 | bytes 11928522 | solution.py:133
  34.9 1.4 reshape.186
  36.3 15.2 %while.47 = (s32[]{:T(128)}, f32[2,128,8,16]{1,0,3,2:T(2,128)S(1)}, f32[2,128,8,16]{1,0,3,2:T(2,128)S(1)}, f32[2,128,8]{1,2,0:T(8,128)S(1)}, s32[2]{0:T(128)S(1)...) while((s32[]{:T(128)}, f32[2,128,8,16]{1,0,3,2:T(2,128)S(1)}, ...), condition=%wide.region_3.3_spmd, body=%wide.region_1.2_spmd.sunk | while | flops 25197572 | bytes 7834299 | solution.py:77
  41.0 1.3 dynamic_update_slice.55
  42.6 1.4 dynamic_update_slice.54
  48.6 1.3 dynamic_update_slice.55
  50.2 1.4 dynamic_update_slice.54
  54.9 1.4 reshape.186
  56.4 15.2 %while.47 = (s32[]{:T(128)}, f32[2,128,8,16]{1,0,3,2:T(2,128)S(1)}, f32[2,128,8,16]{1,0,3,2:T(2,128)S(1)}, f32[2,128,8]{1,2,0:T(8,128)S(1)}, s32[2]{0:T(128)S(1)...) while((s32[]{:T(128)}, f32[2,128,8,16]{1,0,3,2:T(2,128)S(1)}, ...), condition=%wide.region_3.3_spmd, body=%wide.region_1.2_spmd.sunk | while | flops 25197572 | bytes 7834299 | solution.py:77
  61.0 1.3 dynamic_update_slice.55
  62.6 1.4 dynamic_update_slice.54
  68.6 1.3 dynamic_update_slice.55
  70.2 1.4 dynamic_update_slice.54
  75.0 1.4 reshape.186
  76.4 15.2 %while.47 = (s32[]{:T(128)}, f32[2,128,8,16]{1,0,3,2:T(2,128)S(1)}, f32[2,128,8,16]{1,0,3,2:T(2,128)S(1)}, f32[2,128,8]{1,2,0:T(8,128)S(1)}, s32[2]{0:T(128)S(1)...) while((s32[]{:T(128)}, f32[2,128,8,16]{1,0,3,2:T(2,128)S(1)}, ...), condition=%wide.region_3.3_spmd, body=%wide.region_1.2_spmd.sunk | while | flops 25197572 | bytes 7834299 | solution.py:77
  81.0 1.3 dynamic_update_slice.55
  82.6 1.4 dynamic_update_slice.54
  88.6 1.3 dynamic_update_slice.55
  90.2 1.4 dynamic_update_slice.54
  95.0 1.4 reshape.186
  96.4 15.2 %while.47 = (s32[]{:T(128)}, f32[2,128,8,16]{1,0,3,2:T(2,128)S(1)}, f32[2,128,8,16]{1,0,3,2:T(2,128)S(1)}, f32[2,128,8]{1,2,0:T(8,128)S(1)}, s32[2]{0:T(128)S(1)...) while((s32[]{:T(128)}, f32[2,128,8,16]{1,0,3,2:T(2,128)S(1)}, ...), condition=%wide.region_3.3_spmd, body=%wide.region_1.2_spmd.sunk | while | flops 25197572 | bytes 7834299 | solution.py:77
  101.0 1.3 dynamic_update_slice.55
  102.6 1.4 dynamic_update_slice.54
  108.6 1.3 dynamic_update_slice.55
  110.2 1.4 dynamic_update_slice.54
  115.0 1.4 reshape.186
  116.4 15.2 %while.47 = (s32[]{:T(128)}, f32[2,128,8,16]{1,0,3,2:T(2,128)S(1)}, f32[2,128,8,16]{1,0,3,2:T(2,128)S(1)}, f32[2,128,8]{1,2,0:T(8,128)S(1)}, s32[2]{0:T(128)S(1)...) while((s32[]{:T(128)}, f32[2,128,8,16]{1,0,3,2:T(2,128)S(1)}, ...), condition=%wide.region_3.3_spmd, body=%wide.region_1.2_spmd.sunk | while | flops 25197572 | bytes 7834299 | solution.py:77
  121.1 1.3 dynamic_update_slice.55
  122.7 1.4 dynamic_update_slice.54
  128.7 1.3 dynamic_update_slice.55
  130.3 1.4 dynamic_update_slice.54
  135.0 1.4 reshape.186
  136.4 15.2 %while.47 = (s32[]{:T(128)}, f32[2,128,8,16]{1,0,3,2:T(2,128)S(1)}, f32[2,128,8,16]{1,0,3,2:T(2,128)S(1)}, f32[2,128,8]{1,2,0:T(8,128)S(1)}, s32[2]{0:T(128)S(1)...) while((s32[]{:T(128)}, f32[2,128,8,16]{1,0,3,2:T(2,128)S(1)}, ...), condition=%wide.region_3.3_spmd, body=%wide.region_1.2_spmd.sunk | while | flops 25197572 | bytes 7834299 | solution.py:77
  141.1 1.3 dynamic_update_slice.55
  142.7 1.4 dynamic_update_slice.54
  148.7 1.3 dynamic_update_slice.55
  150.3 1.4 dynamic_update_slice.54
  155.0 1.4 reshape.186
  156.5 15.2 %while.47 = (s32[]{:T(128)}, f32[2,128,8,16]{1,0,3,2:T(2,128)S(1)}, f32[2,128,8,16]{1,0,3,2:T(2,128)S(1)}, f32[2,128,8]{1,2,0:T(8,128)S(1)}, s32[2]{0:T(128)S(1)...) while((s32[]{:T(128)}, f32[2,128,8,16]{1,0,3,2:T(2,128)S(1)}, ...), condition=%wide.region_3.3_spmd, body=%wide.region_1.2_spmd.sunk | while | flops 25197572 | bytes 7834299 | solution.py:77
  161.1 1.3 dynamic_update_slice.55
  162.7 1.4 dynamic_update_slice.54
  168.7 1.3 dynamic_update_slice.55
  170.3 1.4 dynamic_update_slice.54
  175.1 1.4 reshape.186
  176.5 15.2 %while.47 = (s32[]{:T(128)}, f32[2,128,8,16]{1,0,3,2:T(2,128)S(1)}, f32[2,128,8,16]{1,0,3,2:T(2,128)S(1)}, f32[2,128,8]{1,2,0:T(8,128)S(1)}, s32[2]{0:T(128)S(1)...) while((s32[]{:T(128)}, f32[2,128,8,16]{1,0,3,2:T(2,128)S(1)}, ...), condition=%wide.region_3.3_spmd, body=%wide.region_1.2_spmd.sunk | while | flops 25197572 | bytes 7834299 | solution.py:77
  181.1 1.3 dynamic_update_slice.55
  182.7 1.4 dynamic_update_slice.54
  188.7 1.3 dynamic_update_slice.55
  190.3 1.4 dynamic_update_slice.54
  193.3 2.7 copy.46
  195.9 1.6 multiply_convert_fusion.1
  197.5 1.6 copy.45
  199.5 1.6 collective-permute-start.3
  201.8 4.0 %fusion.11 = (f32[3,1024]{1,0:T(4,128)S(1)}, f32[3,1024]{1,0:T(4,128)S(1)}, f32[3,1024]{1,0:T(4,128)S(1)}, f32[3,1024]{1,0:T(4,128)S(1)}, f32[3,1024]{1,0:T(4,12...) fusion(f32[256,1024]{1,0:T(8,128)} %get-tuple-element.270, ...), kind=kLoop, calls=%fused_computation.30 | loop fusion | flops 14658560 | bytes 10059776 | tf_op jit(solution)/shard_map/reduce_sum | solution.py:160
  206.3 3.6 %multiply_reduce_fusion.5 = (f32[256,1024]{1,0:T(8,128)S(1)}, f32[256,1024]{1,0:T(8,128)S(1)}, f32[256,1024]{1,0:T(8,128)S(1)}, f32[256,1024]{1,0:T(8,128)S(1)},...) fusion(bf16[3,262,1024]{2,1,0:T(8,128)(2,1)S(1)} %pad_maximum_fusion, f32[3,1024]{1,0:T(4,128)S(1)} %get-tuple-element.300, ...), kind=kLoop, calls=%fused_computation.39 | loop fusion | flops 12582912 | bytes 15802368 | tf_op jit(solution)/shard_map/reduce_sum | solution.py:153
  213.0 75.1 %all_gather.6 = f32[32,21,32,2]{2,3,1,0:T(2,128)S(1)} all-gather(f32[1,21,32,2]{2,3,1,0:T(2,128)S(1)} %copy.49), channel_id=1, replica_groups=mesh['section'=4,'ctx'=32,'dp'=4] {'ctx'}, dimensions={0}, use_global_device_ids=true | all-gather | bytes 177408 | tf_op jit(solution)/shard_map/all_gather | solution.py:19
  289.5 52.6 %all-gather.2.cloned.1.call-done = f32[32,128,32,2]{1,2,3,0:T(8,128)} async-done(((f32[1,128,32,2]{1,2,3,0:T(8,128)}), f32[32,128,32,2]{1,2,3,0:T(8,128)}) %all-gather.2.cloned.1.call-update) | async-done | bytes 1048592 | tf_op jit(solution)/shard_map/all_gather | solution.py:19
  342.1 1.6 dynamic-slice_reduce_fusion.1
  (390 shorter events, 87.9 us)
Async XLA Ops:
  7.2 5.9 %copy-start.7 = (bf16[1,21,64]{2,1,0:T(8,128)(2,1)S(1)}, bf16[1,21,64]{2,1,0:T(8,128)(2,1)}, u32[]{:S(2)}) copy-start(bf16[1,21,64]{2,1,0:T(8,128)(2,1)} %param.10) | copy-start | bytes 8068
  7.2 334.9 %all-gather.2.cloned.1.call-start = ((), (), s32[]{:S(2)}) async-start(), calls=%async_computation | async-start | bytes 1081344 | tf_op jit(solution)/shard_map/all_gather | solution.py:19
  8.0 5.9 %copy-start.4 = (bf16[1,256,1024]{2,1,0:T(8,128)(2,1)S(1)}, bf16[1,256,1024]{2,1,0:T(8,128)(2,1)}, u32[]{:S(2)}) copy-start(bf16[1,256,1024]{2,1,0:T(8,128)(2,1)} %param.8) | copy-start | bytes 1572868
  8.0 5.9 %collective-permute-start.1 = (bf16[6,1024]{1,0:T(8,128)(2,1)S(1)}, bf16[6,1024]{1,0:T(8,128)(2,1)S(1)}, u32[]{:S(2)}, u32[]{:S(2)}) collective-permute-start(bf16[6,1024]{1,0:T(8,128)(2,1)S(1)} %get-tuple-element.286), channel_id=1, source_target_pairs={{0,4},{4,8},{8,12},{12,16},{16,20},{20,24},{24,28},{28,32},{32,36}... | collective-permute-start | bytes 36872 | tf_op jit(solution)/shard_map/ppermute | solution.py:12
  13.1 3.9 %copy-start.2 = (f32[256,1024]{1,0:T(8,128)}, f32[256,1024]{1,0:T(8,128)S(1)}, u32[]{:S(2)}) copy-start(f32[256,1024]{1,0:T(8,128)S(1)} %bitcast_convert_fusion.1) | copy-start | bytes 3145732
  18.8 1.7 copy-start
  18.9 1.4 copy-start.5
  20.5 9.8 %collective-permute-start.2 = (bf16[127,1024]{1,0:T(8,128)(2,1)S(1)}, bf16[127,1024]{1,0:T(8,128)(2,1)S(1)}, u32[]{:S(2)}, u32[]{:S(2)}) collective-permute-start(bf16[127,1024]{1,0:T(8,128)(2,1)S(1)} %slice_bitcast_fusion.1), channel_id=1, source_target_pairs={{4,0},{8,4},{12,8},{16,12},{20,16},{24,20},{28,24},{32,28},{36,32}... | collective-permute-start | bytes 780296 | tf_op jit(solution)/shard_map/ppermute | solution.py:12
  22.0 9.7 %collective-permute-start = (bf16[127,1024]{1,0:T(8,128)(2,1)S(1)}, bf16[127,1024]{1,0:T(8,128)(2,1)S(1)}, u32[]{:S(2)}, u32[]{:S(2)}) collective-permute-start(bf16[127,1024]{1,0:T(8,128)(2,1)S(1)} %slice_bitcast_fusion.2), channel_id=1, source_target_pairs={{0,4},{4,8},{8,12},{12,16},{16,20},{20,24},{24,28},{28,32},{32,36}... | collective-permute-start | bytes 780296 | tf_op jit(solution)/shard_map/ppermute | solution.py:12
  193.3 2.7 copy-start.1
  197.5 1.6 copy-start.6
  199.3 2.5 copy-start.3
  199.5 6.6 %collective-permute-start.3 = (bf16[3,6,1024]{2,1,0:T(8,128)(2,1)S(1)}, bf16[3,6,1024]{2,1,0:T(8,128)(2,1)S(1)}, u32[]{:S(2)}, u32[]{:S(2)}) collective-permute-start(bf16[3,6,1024]{2,1,0:T(8,128)(2,1)S(1)} %slice.262), channel_id=1, source_target_pairs={{4,0},{8,4},{12,8},{16,12},{20,16},{24,20},{28,24},{32,28},{36,32}... | collective-permute-start | bytes 110600 | tf_op jit(solution)/shard_map/ppermute | solution.py:12
  210.7 78.9 %collective-permute-start.4 = (bf16[1,256,1024]{2,1,0:T(8,128)(2,1)S(1)}, bf16[1,256,1024]{2,1,0:T(8,128)(2,1)S(1)}, u32[]{:S(2)}, u32[]{:S(2)}) collective-permute-start(bf16[1,256,1024]{2,1,0:T(8,128)(2,1)S(1)} %fusion.17), channel_id=1, source_target_pairs={{128,0},{256,128},{384,256},{129,1},{257,129},{385,257},{130,2},{2... | collective-permute-start | bytes 1572872 | tf_op jit(solution)/shard_map/ppermute | solution.py:12
Sparse Core Ops, SparseCore 0:
  201.9 140.1 all-gather.1

commit v2 on v1

--- a/solution.py
+++ b/solution.py
@@ -15,10 +15,22 @@
 def owned_sum(partial_terms, axis):
     axis_len = lax.axis_size(axis)
     row_count, col_count = partial_terms.shape
-    blocks = partial_terms.reshape(row_count, axis_len, col_count // axis_len)
-    gathered = lax.all_gather(blocks, axis, axis=0, tiled=False)
-    mine = lax.dynamic_index_in_dim(gathered, lax.axis_index(axis), axis=2, keepdims=False)
-    return jnp.sum(mine, axis=0)
+    width = col_count // axis_len
+    chunks = partial_terms.reshape(row_count, axis_len, width).transpose(1, 2, 0)
+    chunks = chunks.reshape(axis_len, width * row_count)
+    if axis_len & (axis_len - 1):
+        gathered = lax.all_gather(chunks, axis, axis=0, tiled=False)
+        return jnp.sum(gathered[:, lax.axis_index(axis)], axis=0).reshape(width, row_count).T
+    here = lax.axis_index(axis)
+    span = axis_len // 2
+    while span >= 1:
+        upper = (here // span) % 2
+        kept = lax.dynamic_slice_in_dim(chunks, upper * span, span, 0)
+        sent = lax.dynamic_slice_in_dim(chunks, (1 - upper) * span, span, 0)
+        route = [(i, i ^ span) for i in range(axis_len)]
+        chunks = kept + lax.ppermute(sent, axis, route)
+        span //= 2
+    return chunks[0].reshape(width, row_count).T
 
 
 def band_matrix(filter_taps, out_rows):

time: 353 us -> 293 us (0.83)
  the two profiles are of different devices: /device:TPU:8 before, /device:TPU:1 now
where the time goes in v2:
time: 293 us; the launch traced here: 291 us
  local copies, waits for them, and re-layouts  122 us (42%)
  starting transfers between devices  75.8 us (26%)
  loops' own time  32.7 us (11%)
  other arithmetic  23.1 us (8%)
  waiting for transfers between devices  19.6 us (7%)
  matrix products  16 us (5%)
    ppermute x10, starting transfers between devices, owned_sum(): chunks = kept + lax.ppermute(sent, axis, route)  54.2 us
    dynamic_update_slice x48, local copies, waits for them, and re-layouts, medium_block(): mixed_out, back_out, taps_grad = lax.map(row_part, starts)  43.1 us
    another operation x8, loops' own time, medium_block(): mixed_out, back_out, taps_grad = lax.map(row_part, starts)  32.1 us
    ppermute x5, starting transfers between devices, passed_along(): return lax.ppermute(block, axis, route)  21.6 us
    ppermute x10, waiting for transfers between devices, owned_sum(): chunks = kept + lax.ppermute(sent, axis, route)  13.2 us
    squeeze x16, local copies, waits for them, and re-layouts, per_device(): lax.map(partial(medium_block, row_block=row_block), (taps_blocks, split_g...  13.2 us
    reshape x8, local copies, waits for them, and re-layouts, band_matrix(): return tiled_rows.reshape(group_count, out_rows, span_len)  10.9 us
    dynamic_update_slice x24, local copies, waits for them, and re-layouts, per_device(): lax.map(partial(medium_block, row_block=row_block), (taps_blocks, split_g...  10.7 us
  transfers between devices with their start and end apart: 15, of which 8 were waited for; matrix products, arithmetic and copies ran while one was open for 3% of the time, Pallas kernels for 0%

profile of v2, /device:TPU:1, one launch (start us, length us, event | category | flops | bytes accessed | tf_op | source)
XLA Modules:
  0.0 291.0 jit_solution(4118909123296821189)
XLA Ops:
  1.4 4.5 %collective-permute-start.1 = (bf16[6,1024]{1,0:T(8,128)(2,1)S(1)}, bf16[6,1024]{1,0:T(8,128)(2,1)S(1)}, u32[]{:S(2)}, u32[]{:S(2)}) collective-permute-start(bf16[6,1024]{1,0:T(8,128)(2,1)S(1)} %get-tuple-element.286), channel_id=1, source_target_pairs={{0,4},{4,8},{8,12},{12,16},{16,20},{20,24},{24,28},{28,32},{32,36}... | collective-permute-start | bytes 36872 | tf_op jit(solution)/shard_map/ppermute | solution.py:12
  8.0 3.1 %fusion.21 = (f32[256,1024]{1,0:T(8,128)}, f32[256,1024]{1,0:T(8,128)}, f32[256,1024]{1,0:T(8,128)}, f32[256,1024]{1,0:T(8,128)}, f32[256,1024]{1,0:T(8,128)}, /...) fusion(bf16[6,1024]{1,0:T(8,128)(2,1)S(1)} %collective-permute-, ...), kind=kLoop, calls=%fused_computation.66 | loop fusion | flops 7864320 | bytes 13119488 | tf_op jit(solution)/shard_map/convert_element_type | solution.py:174
  11.1 1.5 add_convert_fusion
  16.1 4.2 %collective-permute-start = (bf16[127,1024]{1,0:T(8,128)(2,1)S(1)}, bf16[127,1024]{1,0:T(8,128)(2,1)S(1)}, u32[]{:S(2)}, u32[]{:S(2)}) collective-permute-start(bf16[127,1024]{1,0:T(8,128)(2,1)S(1)} %slice_bitcast_fusion.2), channel_id=1, source_target_pairs={{0,4},{4,8},{8,12},{12,16},{16,20},{20,24},{24,28},{28,32},{32,36}... | collective-permute-start | bytes 780296 | tf_op jit(solution)/shard_map/ppermute | solution.py:12
  20.4 1.6 collective-permute-done.2
  25.0 160.2 %while.46 = (s32[]{:T(128)}, f32[8,256,8,16]{1,3,2,0:T(8,128)}, f32[8,256,8,16]{1,3,2,0:T(8,128)}, f32[8,128,8]{1,2,0:T(8,128)S(1)}, bf16[8,383,8,16]{1,3,2,0:T(...) while((s32[]{:T(128)}, f32[8,256,8,16]{1,3,2,0:T(8,128)}, ...), condition=%wide.region_5.6_spmd, body=%wide.region_0.5_spmd.sunk | while | flops 25198600 | bytes 11928522 | solution.py:145
  26.8 1.4 reshape.200
  28.2 15.2 %while.47 = (s32[]{:T(128)}, f32[2,128,8,16]{1,0,3,2:T(2,128)S(1)}, f32[2,128,8,16]{1,0,3,2:T(2,128)S(1)}, f32[2,128,8]{1,2,0:T(8,128)S(1)}, s32[2]{0:T(128)S(1)...) while((s32[]{:T(128)}, f32[2,128,8,16]{1,0,3,2:T(2,128)S(1)}, ...), condition=%wide.region_3.3_spmd, body=%wide.region_1.2_spmd.sunk | while | flops 25197572 | bytes 7834299 | solution.py:89
  32.8 1.3 dynamic_update_slice.55
  34.4 1.4 dynamic_update_slice.54
  40.4 1.3 dynamic_update_slice.55
  42.0 1.4 dynamic_update_slice.54
  46.8 1.4 reshape.200
  48.2 15.2 %while.47 = (s32[]{:T(128)}, f32[2,128,8,16]{1,0,3,2:T(2,128)S(1)}, f32[2,128,8,16]{1,0,3,2:T(2,128)S(1)}, f32[2,128,8]{1,2,0:T(8,128)S(1)}, s32[2]{0:T(128)S(1)...) while((s32[]{:T(128)}, f32[2,128,8,16]{1,0,3,2:T(2,128)S(1)}, ...), condition=%wide.region_3.3_spmd, body=%wide.region_1.2_spmd.sunk | while | flops 25197572 | bytes 7834299 | solution.py:89
  54.5 1.4 dynamic_update_slice.54
  60.4 1.3 dynamic_update_slice.55
  62.1 1.4 dynamic_update_slice.54
  66.8 1.4 reshape.200
  68.2 15.2 %while.47 = (s32[]{:T(128)}, f32[2,128,8,16]{1,0,3,2:T(2,128)S(1)}, f32[2,128,8,16]{1,0,3,2:T(2,128)S(1)}, f32[2,128,8]{1,2,0:T(8,128)S(1)}, s32[2]{0:T(128)S(1)...) while((s32[]{:T(128)}, f32[2,128,8,16]{1,0,3,2:T(2,128)S(1)}, ...), condition=%wide.region_3.3_spmd, body=%wide.region_1.2_spmd.sunk | while | flops 25197572 | bytes 7834299 | solution.py:89
  74.5 1.4 dynamic_update_slice.54
  82.1 1.4 dynamic_update_slice.54
  86.9 1.4 reshape.200
  88.3 15.2 %while.47 = (s32[]{:T(128)}, f32[2,128,8,16]{1,0,3,2:T(2,128)S(1)}, f32[2,128,8,16]{1,0,3,2:T(2,128)S(1)}, f32[2,128,8]{1,2,0:T(8,128)S(1)}, s32[2]{0:T(128)S(1)...) while((s32[]{:T(128)}, f32[2,128,8,16]{1,0,3,2:T(2,128)S(1)}, ...), condition=%wide.region_3.3_spmd, body=%wide.region_1.2_spmd.sunk | while | flops 25197572 | bytes 7834299 | solution.py:89
  92.9 1.3 dynamic_update_slice.55
  94.5 1.4 dynamic_update_slice.54
  102.1 1.4 dynamic_update_slice.54
  106.9 1.4 reshape.200
  108.3 15.2 %while.47 = (s32[]{:T(128)}, f32[2,128,8,16]{1,0,3,2:T(2,128)S(1)}, f32[2,128,8,16]{1,0,3,2:T(2,128)S(1)}, f32[2,128,8]{1,2,0:T(8,128)S(1)}, s32[2]{0:T(128)S(1)...) while((s32[]{:T(128)}, f32[2,128,8,16]{1,0,3,2:T(2,128)S(1)}, ...), condition=%wide.region_3.3_spmd, body=%wide.region_1.2_spmd.sunk | while | flops 25197572 | bytes 7834299 | solution.py:89
  114.5 1.4 dynamic_update_slice.54
  122.1 1.4 dynamic_update_slice.54
  126.9 1.4 reshape.200
  128.3 15.2 %while.47 = (s32[]{:T(128)}, f32[2,128,8,16]{1,0,3,2:T(2,128)S(1)}, f32[2,128,8,16]{1,0,3,2:T(2,128)S(1)}, f32[2,128,8]{1,2,0:T(8,128)S(1)}, s32[2]{0:T(128)S(1)...) while((s32[]{:T(128)}, f32[2,128,8,16]{1,0,3,2:T(2,128)S(1)}, ...), condition=%wide.region_3.3_spmd, body=%wide.region_1.2_spmd.sunk | while | flops 25197572 | bytes 7834299 | solution.py:89
  134.5 1.4 dynamic_update_slice.54
  142.1 1.4 dynamic_update_slice.54
  146.9 1.4 reshape.200
  148.3 15.2 %while.47 = (s32[]{:T(128)}, f32[2,128,8,16]{1,0,3,2:T(2,128)S(1)}, f32[2,128,8,16]{1,0,3,2:T(2,128)S(1)}, f32[2,128,8]{1,2,0:T(8,128)S(1)}, s32[2]{0:T(128)S(1)...) while((s32[]{:T(128)}, f32[2,128,8,16]{1,0,3,2:T(2,128)S(1)}, ...), condition=%wide.region_3.3_spmd, body=%wide.region_1.2_spmd.sunk | while | flops 25197572 | bytes 7834299 | solution.py:89
  154.6 1.4 dynamic_update_slice.54
  162.2 1.4 dynamic_update_slice.54
  166.9 1.4 reshape.200
  168.3 15.2 %while.47 = (s32[]{:T(128)}, f32[2,128,8,16]{1,0,3,2:T(2,128)S(1)}, f32[2,128,8,16]{1,0,3,2:T(2,128)S(1)}, f32[2,128,8]{1,2,0:T(8,128)S(1)}, s32[2]{0:T(128)S(1)...) while((s32[]{:T(128)}, f32[2,128,8,16]{1,0,3,2:T(2,128)S(1)}, ...), condition=%wide.region_3.3_spmd, body=%wide.region_1.2_spmd.sunk | while | flops 25197572 | bytes 7834299 | solution.py:89
  174.6 1.4 dynamic_update_slice.54
  182.2 1.4 dynamic_update_slice.54
  185.1 2.7 copy.35
  187.8 1.6 multiply_convert_fusion.1
  189.4 2.7 copy.34
  192.1 1.5 fusion.16
  193.9 4.6 %fusion.11 = (f32[3,1024]{1,0:T(4,128)S(1)}, f32[3,1024]{1,0:T(4,128)S(1)}, f32[3,1024]{1,0:T(4,128)S(1)}, f32[3,1024]{1,0:T(4,128)S(1)}, f32[3,1024]{1,0:T(4,12...) fusion(f32[256,1024]{1,0:T(8,128)} %get-tuple-element.270, ...), kind=kLoop, calls=%fused_computation.30 | loop fusion | flops 14658560 | bytes 10059776 | tf_op jit(solution)/shard_map/reduce_sum | solution.py:172
  199.6 13.9 %collective-permute-start.5 = (f32[16,42]{0,1:T(8,128)S(1)}, f32[16,42]{0,1:T(8,128)S(1)}, u32[]{:S(2)}, u32[]{:S(2)}) collective-permute-start(f32[16,42]{0,1:T(8,128)S(1)} %copy.53), channel_id=1, source_target_pairs={{0,64},{4,68},{8,72},{12,76},{16,80},{20,84},{24,88},{28,92},{32,9... | collective-permute-start | bytes 8072 | tf_op jit(solution)/shard_map/ppermute | solution.py:31
  214.8 8.9 %collective-permute-start.6 = (f32[8,42]{0,1:T(8,128)S(1)}, f32[8,42]{0,1:T(8,128)S(1)}, u32[]{:S(2)}, u32[]{:S(2)}) collective-permute-start(f32[8,42]{0,1:T(8,128)S(1)} %constant_dynamic-slice_fusion.12), channel_id=1, source_target_pairs={{0,32},{4,36},{8,40},{12,44},{16,48},{20,52},{24,56},{28,60},{32,0... | collective-permute-start | bytes 4040 | tf_op jit(solution)/shard_map/ppermute | solution.py:31
  223.9 4.3 %collective-permute-done.6 = f32[8,42]{0,1:T(8,128)S(1)} collective-permute-done((f32[8,42]{0,1:T(8,128)S(1)}, f32[8,42]{0,1:T(8,128)S(1)}, u32[]{:S(2)}, u32[]{:S(2)}) %collective-permute-start.6) | collective-permute-done | bytes 1376 | tf_op jit(solution)/shard_map/ppermute | solution.py:31
  228.4 2.0 collective-permute-start.7
  230.4 3.2 %collective-permute-start.10 = (f32[16,256]{1,0:T(8,128)S(1)}, f32[16,256]{1,0:T(8,128)S(1)}, u32[]{:S(2)}, u32[]{:S(2)}) collective-permute-start(f32[16,256]{1,0:T(8,128)S(1)} %constant_dynamic-slice_fusion.8), channel_id=1, source_target_pairs={{0,64},{4,68},{8,72},{12,76},{16,80},{20,84},{24,88},{28,92},{32,9... | collective-permute-start | bytes 49160 | tf_op jit(solution)/shard_map/ppermute | solution.py:31
  234.9 2.0 collective-permute-done.7
  237.0 2.4 collective-permute-start.8
  239.4 8.8 %collective-permute-start.11 = (f32[8,256]{1,0:T(8,128)S(1)}, f32[8,256]{1,0:T(8,128)S(1)}, u32[]{:S(2)}, u32[]{:S(2)}) collective-permute-start(f32[8,256]{1,0:T(8,128)S(1)} %constant_dynamic-slice_fusion.7), channel_id=1, source_target_pairs={{0,32},{4,36},{8,40},{12,44},{16,48},{20,52},{24,56},{28,60},{32,0... | collective-permute-start | bytes 24584 | tf_op jit(solution)/shard_map/ppermute | solution.py:31
  248.3 4.2 %collective-permute-done.11 = f32[8,256]{1,0:T(8,128)S(1)} collective-permute-done((f32[8,256]{1,0:T(8,128)S(1)}, f32[8,256]{1,0:T(8,128)S(1)}, u32[]{:S(2)}, u32[]{:S(2)}) %collective-permute-start.11) | collective-permute-done | bytes 8224 | tf_op jit(solution)/shard_map/ppermute | solution.py:31
  252.5 6.4 %collective-permute-start.12 = (f32[4,256]{1,0:T(4,128)S(1)}, f32[4,256]{1,0:T(4,128)S(1)}, u32[]{:S(2)}, u32[]{:S(2)}) collective-permute-start(f32[4,256]{1,0:T(4,128)S(1)} %constant_dynamic-slice_fusion.5), channel_id=1, source_target_pairs={{0,16},{4,20},{8,24},{12,28},{16,0},{20,4},{24,8},{28,12},{32,48},... | collective-permute-start | bytes 12296 | tf_op jit(solution)/shard_map/ppermute | solution.py:31
  259.0 2.4 collective-permute-start.9
  261.5 4.3 %collective-permute-start.13 = (f32[2,256]{1,0:T(2,128)S(1)}, f32[2,256]{1,0:T(2,128)S(1)}, u32[]{:S(2)}, u32[]{:S(2)}) collective-permute-start(f32[2,256]{1,0:T(2,128)S(1)} %constant_dynamic-slice_fusion.3), channel_id=1, source_target_pairs={{0,8},{4,12},{8,0},{12,4},{16,24},{20,28},{24,16},{28,20},{32,40},... | collective-permute-start | bytes 6152 | tf_op jit(solution)/shard_map/ppermute | solution.py:31
  266.0 3.6 %multiply_reduce_fusion.5 = (f32[256,1024]{1,0:T(8,128)S(1)}, f32[256,1024]{1,0:T(8,128)S(1)}, f32[256,1024]{1,0:T(8,128)S(1)}, f32[256,1024]{1,0:T(8,128)S(1)},...) fusion(bf16[3,262,1024]{2,1,0:T(8,128)(2,1)S(1)} %pad_maximum_fusion, f32[3,1024]{1,0:T(4,128)S(1)} %get-tuple-element.302, ...), kind=kLoop, calls=%fused_computation.39 | loop fusion | flops 12582912 | bytes 15802368 | tf_op jit(solution)/shard_map/reduce_sum | solution.py:165
  270.4 10.4 %collective-permute-start.4 = (bf16[1,256,1024]{2,1,0:T(8,128)(2,1)S(1)}, bf16[1,256,1024]{2,1,0:T(8,128)(2,1)S(1)}, u32[]{:S(2)}, u32[]{:S(2)}) collective-permute-start(bf16[1,256,1024]{2,1,0:T(8,128)(2,1)S(1)} %fusion.17), channel_id=1, source_target_pairs={{128,0},{256,128},{384,256},{129,1},{257,129},{385,257},{130,2},{2... | collective-permute-start | bytes 1572872 | tf_op jit(solution)/shard_map/ppermute | solution.py:12
  280.8 1.9 collective-permute-start.14
  283.6 1.7 collective-permute-done.14
  285.8 4.4 %collective-permute-done.4 = bf16[1,256,1024]{2,1,0:T(8,128)(2,1)S(1)} collective-permute-done((bf16[1,256,1024]{2,1,0:T(8,128)(2,1)S(1)}, bf16[1,256,1024]{2,1,0:T(8,128)(2,1)S(1)}, u32[]{:S(2)}, u32[]{:S(2)}) %collective-permute-start.4) | collective-permute-done | bytes 524320 | tf_op jit(solution)/shard_map/ppermute | solution.py:12
  (432 shorter events, 106.5 us)
Async XLA Ops:
  0.6 6.4 %copy-start.10 = (bf16[1,21,64]{2,1,0:T(8,128)(2,1)S(1)}, bf16[1,21,64]{2,1,0:T(8,128)(2,1)}, u32[]{:S(2)}) copy-start(bf16[1,21,64]{2,1,0:T(8,128)(2,1)} %param.10) | copy-start | bytes 8068
  1.4 6.6 %copy-start.4 = (bf16[1,256,1024]{2,1,0:T(8,128)(2,1)S(1)}, bf16[1,256,1024]{2,1,0:T(8,128)(2,1)}, u32[]{:S(2)}) copy-start(bf16[1,256,1024]{2,1,0:T(8,128)(2,1)} %param.8) | copy-start | bytes 1572868
  1.4 6.6 %collective-permute-start.1 = (bf16[6,1024]{1,0:T(8,128)(2,1)S(1)}, bf16[6,1024]{1,0:T(8,128)(2,1)S(1)}, u32[]{:S(2)}, u32[]{:S(2)}) collective-permute-start(bf16[6,1024]{1,0:T(8,128)(2,1)S(1)} %get-tuple-element.286), channel_id=1, source_target_pairs={{0,4},{4,8},{8,12},{12,16},{16,20},{20,24},{24,28},{28,32},{32,36}... | collective-permute-start | bytes 36872 | tf_op jit(solution)/shard_map/ppermute | solution.py:12
  7.1 4.0 %copy-start.2 = (f32[256,1024]{1,0:T(8,128)}, f32[256,1024]{1,0:T(8,128)S(1)}, u32[]{:S(2)}) copy-start(f32[256,1024]{1,0:T(8,128)S(1)} %bitcast_convert_fusion.1) | copy-start | bytes 3145732
  13.0 1.7 copy-start
  13.0 1.4 copy-start.8
  14.6 7.3 %collective-permute-start.2 = (bf16[127,1024]{1,0:T(8,128)(2,1)S(1)}, bf16[127,1024]{1,0:T(8,128)(2,1)S(1)}, u32[]{:S(2)}, u32[]{:S(2)}) collective-permute-start(bf16[127,1024]{1,0:T(8,128)(2,1)S(1)} %slice_bitcast_fusion.1), channel_id=1, source_target_pairs={{4,0},{8,4},{12,8},{16,12},{20,16},{24,20},{28,24},{32,28},{36,32}... | collective-permute-start | bytes 780296 | tf_op jit(solution)/shard_map/ppermute | solution.py:12
  16.1 7.5 %collective-permute-start = (bf16[127,1024]{1,0:T(8,128)(2,1)S(1)}, bf16[127,1024]{1,0:T(8,128)(2,1)S(1)}, u32[]{:S(2)}, u32[]{:S(2)}) collective-permute-start(bf16[127,1024]{1,0:T(8,128)(2,1)S(1)} %slice_bitcast_fusion.2), channel_id=1, source_target_pairs={{0,4},{4,8},{8,12},{12,16},{16,20},{20,24},{24,28},{28,32},{32,36}... | collective-permute-start | bytes 780296 | tf_op jit(solution)/shard_map/ppermute | solution.py:12
  185.1 2.7 copy-start.1
  189.4 2.7 copy-start.9
  189.4 4.2 %copy-start.3 = (f32[256,1024]{1,0:T(8,128)S(1)}, f32[256,1024]{1,0:T(8,128)}, u32[]{:S(2)}) copy-start(f32[256,1024]{1,0:T(8,128)} %copy-done.2) | copy-start | bytes 3145732
  192.1 1.5 copy-start.6
  192.1 1.9 copy-start.7
  199.6 15.1 %collective-permute-start.5 = (f32[16,42]{0,1:T(8,128)S(1)}, f32[16,42]{0,1:T(8,128)S(1)}, u32[]{:S(2)}, u32[]{:S(2)}) collective-permute-start(f32[16,42]{0,1:T(8,128)S(1)} %copy.53), channel_id=1, source_target_pairs={{0,64},{4,68},{8,72},{12,76},{16,80},{20,84},{24,88},{28,92},{32,9... | collective-permute-start | bytes 8072 | tf_op jit(solution)/shard_map/ppermute | solution.py:31
  214.8 13.4 %collective-permute-start.6 = (f32[8,42]{0,1:T(8,128)S(1)}, f32[8,42]{0,1:T(8,128)S(1)}, u32[]{:S(2)}, u32[]{:S(2)}) collective-permute-start(f32[8,42]{0,1:T(8,128)S(1)} %constant_dynamic-slice_fusion.12), channel_id=1, source_target_pairs={{0,32},{4,36},{8,40},{12,44},{16,48},{20,52},{24,56},{28,60},{32,0... | collective-permute-start | bytes 4040 | tf_op jit(solution)/shard_map/ppermute | solution.py:31
  228.4 8.5 %collective-permute-start.7 = (f32[4,42]{0,1:T(8,128)S(1)}, f32[4,42]{0,1:T(8,128)S(1)}, u32[]{:S(2)}, u32[]{:S(2)}) collective-permute-start(f32[4,42]{0,1:T(8,128)S(1)} %constant_dynamic-slice_fusion.11), channel_id=1, source_target_pairs={{0,16},{4,20},{8,24},{12,28},{16,0},{20,4},{24,8},{28,12},{32,48},... | collective-permute-start | bytes 2024 | tf_op jit(solution)/shard_map/ppermute | solution.py:31
  230.4 9.0 %collective-permute-start.10 = (f32[16,256]{1,0:T(8,128)S(1)}, f32[16,256]{1,0:T(8,128)S(1)}, u32[]{:S(2)}, u32[]{:S(2)}) collective-permute-start(f32[16,256]{1,0:T(8,128)S(1)} %constant_dynamic-slice_fusion.8), channel_id=1, source_target_pairs={{0,64},{4,68},{8,72},{12,76},{16,80},{20,84},{24,88},{28,92},{32,9... | collective-permute-start | bytes 49160 | tf_op jit(solution)/shard_map/ppermute | solution.py:31
  233.6 32.2 %collective-permute-start.3 = (bf16[3,6,1024]{2,1,0:T(8,128)(2,1)S(1)}, bf16[3,6,1024]{2,1,0:T(8,128)(2,1)S(1)}, u32[]{:S(2)}, u32[]{:S(2)}) collective-permute-start(bf16[3,6,1024]{2,1,0:T(8,128)(2,1)S(1)} %slice.262), channel_id=1, source_target_pairs={{4,0},{8,4},{12,8},{16,12},{20,16},{24,20},{28,24},{32,28},{36,32}... | collective-permute-start | bytes 110600 | tf_op jit(solution)/shard_map/ppermute | solution.py:12
  237.0 11.3 %collective-permute-start.8 = (f32[2,42]{0,1:T(8,128)S(1)}, f32[2,42]{0,1:T(8,128)S(1)}, u32[]{:S(2)}, u32[]{:S(2)}) collective-permute-start(f32[2,42]{0,1:T(8,128)S(1)} %constant_dynamic-slice_fusion.10), channel_id=1, source_target_pairs={{0,8},{4,12},{8,0},{12,4},{16,24},{20,28},{24,16},{28,20},{32,40},... | collective-permute-start | bytes 1016 | tf_op jit(solution)/shard_map/ppermute | solution.py:31
  239.4 13.1 %collective-permute-start.11 = (f32[8,256]{1,0:T(8,128)S(1)}, f32[8,256]{1,0:T(8,128)S(1)}, u32[]{:S(2)}, u32[]{:S(2)}) collective-permute-start(f32[8,256]{1,0:T(8,128)S(1)} %constant_dynamic-slice_fusion.7), channel_id=1, source_target_pairs={{0,32},{4,36},{8,40},{12,44},{16,48},{20,52},{24,56},{28,60},{32,0... | collective-permute-start | bytes 24584 | tf_op jit(solution)/shard_map/ppermute | solution.py:31
  252.5 8.9 %collective-permute-start.12 = (f32[4,256]{1,0:T(4,128)S(1)}, f32[4,256]{1,0:T(4,128)S(1)}, u32[]{:S(2)}, u32[]{:S(2)}) collective-permute-start(f32[4,256]{1,0:T(4,128)S(1)} %constant_dynamic-slice_fusion.5), channel_id=1, source_target_pairs={{0,16},{4,20},{8,24},{12,28},{16,0},{20,4},{24,8},{28,12},{32,48},... | collective-permute-start | bytes 12296 | tf_op jit(solution)/shard_map/ppermute | solution.py:31
  259.0 23.7 %collective-permute-start.9 = (f32[1,42]{0,1:T(8,128)S(1)}, f32[1,42]{0,1:T(8,128)S(1)}, u32[]{:S(2)}, u32[]{:S(2)}) collective-permute-start(f32[1,42]{0,1:T(8,128)S(1)} %constant_dynamic-slice_fusion.9), channel_id=1, source_target_pairs={{0,4},{4,0},{8,12},{12,8},{16,20},{20,16},{24,28},{28,24},{32,36},... | collective-permute-start | bytes 512 | tf_op jit(solution)/shard_map/ppermute | solution.py:31
  261.5 19.2 %collective-permute-start.13 = (f32[2,256]{1,0:T(2,128)S(1)}, f32[2,256]{1,0:T(2,128)S(1)}, u32[]{:S(2)}, u32[]{:S(2)}) collective-permute-start(f32[2,256]{1,0:T(2,128)S(1)} %constant_dynamic-slice_fusion.3), channel_id=1, source_target_pairs={{0,8},{4,12},{8,0},{12,4},{16,24},{20,28},{24,16},{28,20},{32,40},... | collective-permute-start | bytes 6152 | tf_op jit(solution)/shard_map/ppermute | solution.py:31
  266.0 3.6 %copy-start.5 = (f32[256,1024]{1,0:T(8,128)S(1)}, f32[256,1024]{1,0:T(8,128)}, u32[]{:S(2)}) copy-start(f32[256,1024]{1,0:T(8,128)} %get-tuple-element.266) | copy-start | bytes 3145732
  270.4 19.8 %collective-permute-start.4 = (bf16[1,256,1024]{2,1,0:T(8,128)(2,1)S(1)}, bf16[1,256,1024]{2,1,0:T(8,128)(2,1)S(1)}, u32[]{:S(2)}, u32[]{:S(2)}) collective-permute-start(bf16[1,256,1024]{2,1,0:T(8,128)(2,1)S(1)} %fusion.17), channel_id=1, source_target_pairs={{128,0},{256,128},{384,256},{129,1},{257,129},{385,257},{130,2},{2... | collective-permute-start | bytes 1572872 | tf_op jit(solution)/shard_map/ppermute | solution.py:12
  280.8 4.5 %collective-permute-start.14 = (f32[1,256]{1,0:T(1,128)S(1)}, f32[1,256]{1,0:T(1,128)S(1)}, u32[]{:S(2)}, u32[]{:S(2)}) collective-permute-start(f32[1,256]{1,0:T(1,128)S(1)} %constant_dynamic-slice_fusion.1), channel_id=1, source_target_pairs={{0,4},{4,0},{8,12},{12,8},{16,20},{20,16},{24,28},{28,24},{32,36},... | collective-permute-start | bytes 3080 | tf_op jit(solution)/shard_map/ppermute | solution.py:31
